TPU v7x, 512 devices: a whole 4x8x8 slice. The times are simulated.
512 devices in a mesh: req: 64 (over x, z, core), tp: 8 (over y).
Axes of the slice: x: 4, y: 8, z: 8, core: 2. Of those that a mesh axis runs over, the one named last changes fastest.
Arguments:
- queries: bfloat16 [1280, 2048], P('req', 'tp')
- new_keys: bfloat16 [1280, 2048], P('req', 'tp'), may hold values from -6 to 6
- new_values: bfloat16 [1280, 2048], P('req', 'tp'), may hold values from -6 to 6
- cache_keys: bfloat16 [256, 384, 2048], P('req', None, 'tp'), may hold values from -6 to 6
- cache_values: bfloat16 [256, 384, 2048], P('req', None, 'tp'), may hold values from -6 to 6
- cache_lengths: int32 [256], P('req'), may hold values from 1 to 384, as said below
- hidden_in: bfloat16 [1280, 2048], P('req'), may hold values from -6 to 6
- out_weight: bfloat16 [2048, 2048], P('tp'), may hold values from -0.125 to 0.125
- norm_gain: float32 [2048], replicated, may hold values from 0.25 to 1.75
- routes: int32 [1280, 6], P('req'), may hold values from 0 to 63, all different within a row; in each aligned block of 20 rows (0 to 19, 20 to 39, ...) at most 3 rows name the same one
- route_gates: float32 [1280, 6], P('req'), may hold values from 0.05 to 0.5
- gate_weight: bfloat16 [64, 2048, 1408], P('req', None, 'tp'), may hold values from -0.125 to 0.125
- up_weight: bfloat16 [64, 2048, 1408], P('req', None, 'tp'), may hold values from -0.125 to 0.125
- down_weight: bfloat16 [64, 1408, 2048], P('req', 'tp'), may hold values from -0.15625 to 0.15625
Outputs:
- hidden_out: bfloat16 [1280, 2048], P('req', 'tp')
Inputs may be any that keep to these rules, and one draw needn't show every extreme that they name: `cache_lengths`: at least one request has all 384 slots live. `routes`: each token names 6 different experts; within each aligned block of 20 tokens (the tokens of one index of req) no expert is named more than 3 times.
All inputs are finite; a program needn't handle non-finite values.
Results may differ from a plain program's by a relative error of at most 0.008.
Values may be sent and summed in bfloat16 or wider, within the bound.
No kernel may reach another device: no remote copies, remote signals or barrier semaphores. Data moves between devices by JAX's collectives and lax.ppermute only.
A program may use at most 64 MiB of HBM per device.

v0:
```python
import jax
import jax.numpy as jnp
from jax import lax
from jax.sharding import PartitionSpec as P

HD = 128
EXPERTS = 64
POS = 5
CACHE = 384
CAP = 3


def slot_tables(local_routes, local_gates):
    flat_routes = local_routes.reshape(-1)
    expert_ids = jnp.arange(EXPERTS, dtype=jnp.int32)
    onehot = (flat_routes[:, None] == expert_ids[None, :]).astype(jnp.int32)
    before = jnp.cumsum(onehot, axis=0) - onehot
    ranks = jnp.sum(before * onehot, axis=1)
    slot_ids = (flat_routes * CAP + ranks).reshape(local_routes.shape)
    slot_range = jnp.arange(EXPERTS * CAP, dtype=jnp.int32)
    matches = slot_ids[None, :, :] == slot_range[:, None, None]
    dispatch = jnp.any(matches, axis=-1).astype(jnp.bfloat16)
    combine = jnp.sum(jnp.where(matches, local_gates[None, :, :], 0.0), axis=-1).T
    return (dispatch, combine)


def attend_local(queries, new_keys, new_values, cache_keys, cache_values, cache_lengths):
    req_count = cache_keys.shape[0]
    head_count = queries.shape[1] // HD
    all_keys = jnp.concatenate([cache_keys, new_keys.reshape(req_count, POS, -1)], axis=1).reshape(
        req_count, CACHE + POS, head_count, HD
    )
    all_values = jnp.concatenate(
        [cache_values, new_values.reshape(req_count, POS, -1)], axis=1
    ).reshape(req_count, CACHE + POS, head_count, HD)
    local_q = queries.reshape(req_count, POS, head_count, HD)
    scores = jnp.einsum(
        "rphd,rjhd->rhpj", local_q, all_keys, preferred_element_type=jnp.float32
    ) * HD ** (-0.5)
    key_pos = jnp.arange(CACHE + POS, dtype=jnp.int32)
    query_pos = jnp.arange(POS, dtype=jnp.int32)
    cache_live = key_pos[None, None, :] < cache_lengths[:, None, None]
    fresh_live = key_pos[None, None, :] - CACHE <= query_pos[None, :, None]
    live = jnp.where(key_pos[None, None, :] < CACHE, cache_live, fresh_live)
    scores = jnp.where(live[:, None, :, :], scores, -1e30)
    top = jnp.max(scores, axis=-1, keepdims=True)
    expo = jnp.exp(scores - top)
    weights = (expo / jnp.sum(expo, axis=-1, keepdims=True)).astype(jnp.bfloat16)
    attended = jnp.einsum(
        "rhpj,rjhd->rphd", weights, all_values, preferred_element_type=jnp.float32
    )
    return attended.astype(jnp.bfloat16).reshape(req_count * POS, head_count * HD)


def expert_apply(slot_rows, gate_weight, up_weight, down_weight):
    gated = jnp.einsum("secd,edf->secf", slot_rows, gate_weight, preferred_element_type=jnp.float32)
    upward = jnp.einsum("secd,edf->secf", slot_rows, up_weight, preferred_element_type=jnp.float32)
    activation = (jax.nn.silu(gated) * upward).astype(jnp.bfloat16)
    return jnp.einsum("secf,efd->secd", activation, down_weight, preferred_element_type=jnp.float32)


def local(
    queries,
    new_keys,
    new_values,
    cache_keys,
    cache_values,
    cache_lengths,
    hidden_in,
    out_weight,
    norm_gain,
    routes,
    route_gates,
    gate_weight,
    up_weight,
    down_weight,
):
    attended = attend_local(queries, new_keys, new_values, cache_keys, cache_values, cache_lengths)
    partial_value = jnp.dot(attended, out_weight, preferred_element_type=jnp.float32)
    model_width = partial_value.shape[1]
    tp_count = lax.axis_size("tp")
    columns = model_width // tp_count
    offset = lax.axis_index("tp") * columns
    holders = lax.axis_size("req")
    dispatch, combine = slot_tables(routes, route_gates)
    summed = lax.psum(partial_value, "tp") + hidden_in.astype(jnp.float32)
    mean_square = jnp.mean(summed * summed, axis=-1, keepdims=True)
    normed = (summed * lax.rsqrt(mean_square + 1e-06) * norm_gain[None, :]).astype(jnp.bfloat16)
    outbound = jnp.dot(dispatch, normed, preferred_element_type=jnp.float32).astype(jnp.bfloat16)
    outbound = outbound.reshape(holders, -1, CAP, model_width)
    produced = expert_apply(
        lax.all_to_all(outbound, "req", split_axis=0, concat_axis=0, tiled=True),
        gate_weight,
        up_weight,
        down_weight,
    )
    returned = lax.all_to_all(
        produced.astype(jnp.bfloat16), "req", split_axis=0, concat_axis=0, tiled=True
    ).astype(produced.dtype)
    expert_sum = jnp.dot(
        combine,
        returned.reshape(-1, model_width),
        precision=lax.Precision.HIGHEST,
        preferred_element_type=jnp.float32,
    )
    expert_cols = lax.psum_scatter(
        expert_sum.astype(jnp.bfloat16), "tp", scatter_dimension=1, tiled=True
    ).astype(jnp.float32)
    summed_cols = lax.dynamic_slice_in_dim(summed, offset, columns, 1)
    return (summed_cols + expert_cols).astype(jnp.bfloat16)


def solution(mesh):
    in_specs = (
        P("req", "tp"),
        P("req", "tp"),
        P("req", "tp"),
        P("req", None, "tp"),
        P("req", None, "tp"),
        P("req"),
        P("req", None),
        P("tp", None),
        P(),
        P("req", None),
        P("req", None),
        P("req", None, "tp"),
        P("req", None, "tp"),
        P("req", "tp", None),
    )
    out_specs = P("req", "tp")
    return jax.shard_map(local, mesh=mesh, in_specs=in_specs, out_specs=out_specs, check_vma=False)
```

profile of v0, /device:TPU:2, one launch (start us, length us, event | category | flops | bytes accessed | tf_op | source)
XLA Modules:
  0.0 220.3 jit_solution(8481350041058466535)
XLA Ops:
  6.5 0.0 copy-start
  6.5 0.0 all-reduce.2.cloned.1.call-start
  6.5 1.6 copy.64
  8.1 0.0 copy-start.4
  8.1 0.0 copy-start.9
  8.2 0.0 copy-start.5
  8.2 0.0 copy-start.1
  8.2 0.4 copy.65
  8.6 0.2 copy-done.4
  8.9 0.0 copy-done.9
  8.9 0.1 iota_compare_fusion.3
  9.0 0.0 copy-done.5
  9.0 0.3 copy-done.1
  9.3 0.4 copy.61
  9.7 0.0 copy-start.6
  9.7 0.4 copy.62
  10.1 0.3 copy-done.6
  10.4 0.6 fusion.71
  11.0 0.6 fusion.9
  11.6 0.0 copy-start.3
  11.6 0.0 copy-start.2
  11.7 0.0 copy-done
  11.7 0.0 copy-start.7
  11.7 0.9 fusion.76
  12.6 0.0 all-reduce.2.cloned.1.call-update
  12.7 0.0 copy-done.3
  12.7 0.1 copy.69
  12.8 0.1 eq.28
  12.9 0.1 fusion.38
  13.0 0.2 reduce_window_sum.11
  13.1 0.2 select_reduce_fusion.1
  13.3 0.1 reduce_sum.40
  13.4 0.1 copy.70
  13.5 0.1 fusion.33
  13.6 81.7 %all-reduce.2.cloned.1.call-done = f32[20,2048]{1,0:T(8,128)} async-done(((f32[20,2048]{1,0:T(8,128)}), f32[20,2048]{1,0:T(8,128)}) %all-reduce.2.cloned.1.call-update) | async-done | bytes 163856 | tf_op jit(solution)/shard_map/psum | solution.py:86
  95.3 0.0 copy-done.2
  95.3 1.1 multiply_reduce_fusion
  96.4 0.0 copy-done.7
  96.4 0.4 convolution_convert_fusion.1
  96.8 0.5 reshape.120
  97.4 0.0 copy-start.10
  97.4 37.8 %all_to_all.10 = bf16[64,1,3,2048]{3,2,1,0:T(4,128)(2,1)S(1)} all-to-all(bf16[64,1,3,2048]{3,2,1,0:T(4,128)(2,1)S(1)} %bitcast.79), channel_id=1, replica_groups=mesh['req'=64,'tp'=8] {'req'}, dimensions={0} | all-to-all | bytes 1572864 | tf_op jit(solution)/shard_map/all_to_all | solution.py:92
  135.2 0.0 copy-done.10
  135.2 1.0 convolution_bitcast_fusion.1
  136.2 2.6 %fusion.1 = bf16[64,1,3,2048]{3,0,2,1:T(8,128)(2,1)S(1)} fusion(bf16[1,176,2048]{2,1,0:T(8,128)(2,1)} %param.27, bf16[1,2048,176]{1,2,0:T(8,128)(2,1)} %param.26, bf16[64,1,3,2048]{3,2,1,0:T(4,128)(2,1)S(1)} %all_to_all.10, f32[64,1,3,176]{3,0,2,1:T(8,128)S(1)} %convolution_bitcast_fusion.1), kind=kOutput, calls=%fused_computation.3 | convolution fusion | flops 277420032 | bytes 3149824 | tf_op jit(solution)/shard_map/secf,efd->secd/dot_general | solution.py:59
  138.8 1.7 copy.73
  140.5 0.0 copy-start.8
  140.5 7.9 %all-to-all-start.1 = ((bf16[64,1,3,2048]{3,2,1,0:T(4,128)(2,1)}), bf16[64,1,3,2048]{3,2,1,0:T(4,128)(2,1)S(1)}, u32[]{:S(2)}, u32[]{:S(2)}) async-start(bf16[64,1,3,2048]{3,2,1,0:T(4,128)(2,1)} %copy.73), calls=%async_computation.1 | async-start | bytes 2097152 | tf_op jit(solution)/shard_map/all_to_all | solution.py:97
  148.4 0.0 reduce-scatter.2.cloned.1.call-start
  148.4 0.0 copy-done.8
  148.4 0.1 select_reduce_fusion
  148.5 26.8 %all-to-all-done.1 = bf16[64,1,3,2048]{3,2,1,0:T(4,128)(2,1)S(1)} async-done(((bf16[64,1,3,2048]{3,2,1,0:T(4,128)(2,1)}), bf16[64,1,3,2048]{3,2,1,0:T(4,128)(2,1)S(1)}, u32[]{:S(2)}, u32[]{:S(2)}) %all-to-all-start.1) | async-done | bytes 786464 | tf_op jit(solution)/shard_map/all_to_all | solution.py:97
  175.3 0.7 reshape.126
  176.0 1.1 convolution_convert_fusion.2
  177.1 0.0 reduce-scatter.2.cloned.1.call-update
  177.1 35.1 %reduce-scatter.2.cloned.1.call-done = bf16[20,256]{1,0:T(8,128)(2,1)} async-done(((bf16[20,2048]{1,0:T(8,128)(2,1)}), bf16[20,256]{1,0:T(8,128)(2,1)}) %reduce-scatter.2.cloned.1.call-update) | async-done | bytes 10256 | tf_op jit(solution)/shard_map/reduce_scatter | solution.py:106
  212.2 1.3 add_convert_fusion
  (14 shorter events, 0.2 us)
Async XLA Ops:
  6.5 5.2 %copy-start = (bf16[256,2048]{1,0:T(8,128)(2,1)S(1)}, bf16[256,2048]{1,0:T(8,128)(2,1)}, u32[]{:S(2)}) copy-start(bf16[256,2048]{1,0:T(8,128)(2,1)} %param.21) | copy-start | bytes 3145732
  6.5 88.8 %all-reduce.2.cloned.1.call-start = ((), (), s32[]{:S(2)}) async-start(), calls=%async_computation.3 | async-start | bytes 393216 | tf_op jit(solution)/shard_map/psum | solution.py:86
  8.1 0.7 copy-start.4
  8.1 0.7 copy-start.9
  8.2 0.8 copy-start.5
  8.2 1.1 copy-start.1
  9.7 0.7 copy-start.6
  11.6 1.1 copy-start.3
  11.6 83.7 %copy-start.2 = (bf16[20,2048]{1,0:T(8,128)(2,1)S(1)}, bf16[20,2048]{1,0:T(8,128)(2,1)}, u32[]{:S(2)}) copy-start(bf16[20,2048]{1,0:T(8,128)(2,1)} %param.20) | copy-start | bytes 245764
  11.7 84.7 %copy-start.7 = (f32[2048]{0:T(1024)S(1)}, f32[2048]{0:T(1024)}, u32[]{:S(2)}) copy-start(f32[2048]{0:T(1024)} %param.22) | copy-start | bytes 24580
  97.4 37.8 %copy-start.10 = (bf16[1,2048,176]{1,2,0:T(8,128)(2,1)S(1)}, bf16[1,2048,176]{1,2,0:T(8,128)(2,1)}, u32[]{:S(2)}) copy-start(bf16[1,2048,176]{1,2,0:T(8,128)(2,1)} %param.25) | copy-start | bytes 2162692
  140.5 8.0 %copy-start.8 = (f32[20,6]{0,1:T(8,128)S(1)}, f32[20,6]{0,1:T(8,128)}, u32[]{:S(2)}) copy-start(f32[20,6]{0,1:T(8,128)} %param.24) | copy-start | bytes 1444
  140.5 34.9 %all-to-all-start.1 = ((bf16[64,1,3,2048]{3,2,1,0:T(4,128)(2,1)}), bf16[64,1,3,2048]{3,2,1,0:T(4,128)(2,1)S(1)}, u32[]{:S(2)}, u32[]{:S(2)}) async-start(bf16[64,1,3,2048]{3,2,1,0:T(4,128)(2,1)} %copy.73), calls=%async_computation.1 | async-start | bytes 2097152 | tf_op jit(solution)/shard_map/all_to_all | solution.py:97
  148.4 63.8 %reduce-scatter.2.cloned.1.call-start = ((), (), s32[]{:S(2)}) async-start(), calls=%async_computation.4 | async-start | bytes 110592 | tf_op jit(solution)/shard_map/reduce_scatter | solution.py:106
Sparse Core Ops, SparseCore 0:
  12.8 82.4 all-reduce.1
  177.2 34.9 reduce-scatter.1
where the time goes:
time: 221 us; the launch traced here: 220 us
  waiting for transfers between devices  144 us (65%)
  blocking collectives  37.8 us (17%)
  between operations  13.7 us (6%)
  starting transfers between devices  7.95 us (4%)
  matrix products  7.21 us (3%)
  local copies, waits for them, and re-layouts  6.98 us (3%)
  other arithmetic  3.12 us (1%)
    psum x1, waiting for transfers between devices, local(): summed = lax.psum(partial_value, 'tp') + hidden_in.astype(jnp.float32)  81.7 us
    all_to_all x1, blocking collectives, local(): lax.all_to_all(outbound, 'req', split_axis=0, concat_axis=0, tiled=True)  37.8 us
    reduce_scatter x1, waiting for transfers between devices, local(): lax.psum_scatter(expert_sum.astype(jnp.bfloat16), 'tp', scatter_dimension...  35.1 us
    all_to_all x1, waiting for transfers between devices, local(): lax.all_to_all(produced.astype(jnp.bfloat16), 'req', split_axis=0, concat...  26.8 us
    all_to_all x1, starting transfers between devices, local(): lax.all_to_all(produced.astype(jnp.bfloat16), 'req', split_axis=0, concat...  7.9 us
  transfers between devices with their start and end apart: 3, of which 3 were waited for; matrix products, arithmetic and copies ran while one was open for 0% of the time, Pallas kernels for 0%

commit v1 on v0

--- a/solution.py
+++ b/solution.py
@@ -83,7 +83,7 @@
     offset = lax.axis_index("tp") * columns
     holders = lax.axis_size("req")
     dispatch, combine = slot_tables(routes, route_gates)
-    summed = lax.psum(partial_value, "tp") + hidden_in.astype(jnp.float32)
+    summed = jnp.sum(lax.all_gather(partial_value, "tp"), axis=0) + hidden_in.astype(jnp.float32)
     mean_square = jnp.mean(summed * summed, axis=-1, keepdims=True)
     normed = (summed * lax.rsqrt(mean_square + 1e-06) * norm_gain[None, :]).astype(jnp.bfloat16)
     outbound = jnp.dot(dispatch, normed, preferred_element_type=jnp.float32).astype(jnp.bfloat16)

time: 221 us -> 185 us (0.84)
  waiting for transfers between devices: 144 us -> 108 us
    psum x1 -> x0, waiting for transfers between devices: 81.7 us -> none  [local(): summed = lax.psum(partial_value, 'tp') + hidden_in.astype(jnp.float32)]
    all_gather x0 -> x1, waiting for transfers between devices: none -> 45.9 us  [local(): lax.all_gather(partial_value, 'tp')]
  transfers between devices with their start and end apart: 3 -> 3, of which waited for: 3 -> 3; matrix products, arithmetic and copies ran while one was open for 0% -> 1% of each run, Pallas kernels for 0% -> 0%
where the time goes in v1:
time: 185 us; the launch traced here: 184 us
  waiting for transfers between devices  108 us (58%)
  blocking collectives  37.8 us (20%)
  between operations  13.7 us (7%)
  starting transfers between devices  7.82 us (4%)
  matrix products  7.2 us (4%)
  local copies, waits for them, and re-layouts  6.22 us (3%)
  other arithmetic  3.72 us (2%)
    all_gather x1, waiting for transfers between devices, local(): lax.all_gather(partial_value, 'tp')  45.9 us
    all_to_all x1, blocking collectives, local(): lax.all_to_all(outbound, 'req', split_axis=0, concat_axis=0, tiled=True)  37.8 us
    reduce_scatter x1, waiting for transfers between devices, local(): lax.psum_scatter(expert_sum.astype(jnp.bfloat16), 'tp', scatter_dimension...  35.2 us
    all_to_all x1, waiting for transfers between devices, local(): lax.all_to_all(produced.astype(jnp.bfloat16), 'req', split_axis=0, concat...  26.8 us
    all_to_all x1, starting transfers between devices, local(): lax.all_to_all(produced.astype(jnp.bfloat16), 'req', split_axis=0, concat...  7.77 us
  transfers between devices with their start and end apart: 3, of which 3 were waited for; matrix products, arithmetic and copies ran while one was open for 1% of the time, Pallas kernels for 0%

profile of v1, /device:TPU:2, one launch (start us, length us, event | category | flops | bytes accessed | tf_op | source)
XLA Modules:
  0.0 184.3 jit_solution(8068088640754788358)
XLA Ops:
  6.5 0.0 copy-start
  6.5 0.0 all-gather.4.cloned.1.call-start
  6.5 0.0 copy-start.4
  6.6 0.0 copy-start.9
  6.6 0.0 copy-start.5
  6.6 0.0 copy-start.1
  6.6 1.6 copy.64
  8.2 0.4 copy.65
  8.6 0.0 copy-done.4
  8.7 0.0 copy-done.9
  8.7 0.1 iota_compare_fusion.3
  8.8 0.0 copy-done.5
  8.8 0.0 copy-done.1
  8.8 0.0 copy-start.6
  8.8 0.4 copy.61
  9.2 0.5 copy.62
  9.6 0.0 copy-done.6
  9.7 0.6 fusion.71
  10.3 0.0 copy-start.3
  10.3 0.6 fusion.9
  10.9 0.0 copy-done
  11.0 0.0 copy-start.2
  11.0 0.9 convolution_bitcast_fusion
  11.9 0.0 copy-start.7
  11.9 0.0 all-gather.4.cloned.1.call-update
  11.9 0.0 copy-done.3
  11.9 0.1 copy.69
  12.0 0.1 eq.28
  12.1 0.1 fusion.38
  12.2 0.2 reduce_window_sum.11
  12.4 0.2 select_reduce_fusion.1
  12.6 0.1 reduce_sum.50
  12.7 0.1 copy.70
  12.8 0.1 fusion.33
  12.9 45.9 %all-gather.4.cloned.1.call-done = f32[8,20,2048]{2,1,0:T(8,128)} async-done(((f32[1,20,2048]{2,1,0:T(8,128)}), f32[8,20,2048]{2,1,0:T(8,128)}) %all-gather.4.cloned.1.call-update) | async-done | bytes 1310736 | tf_op jit(solution)/shard_map/all_gather | solution.py:86
  58.7 1.5 reduce_sum.48
  60.2 0.0 copy-done.2
  60.2 0.1 multiply_reduce_fusion
  60.4 0.0 copy-done.7
  60.4 0.4 convolution_convert_fusion.1
  60.8 0.5 reshape.120
  61.4 0.0 copy-start.10
  61.4 37.8 %all_to_all.10 = bf16[64,1,3,2048]{3,2,1,0:T(4,128)(2,1)S(1)} all-to-all(bf16[64,1,3,2048]{3,2,1,0:T(4,128)(2,1)S(1)} %bitcast.81), channel_id=1, replica_groups=mesh['req'=64,'tp'=8] {'req'}, dimensions={0} | all-to-all | bytes 1572864 | tf_op jit(solution)/shard_map/all_to_all | solution.py:92
  99.2 0.0 copy-done.10
  99.2 1.0 convolution_bitcast_fusion.2
  100.2 2.6 %fusion.1 = bf16[64,1,3,2048]{3,0,2,1:T(8,128)(2,1)S(1)} fusion(bf16[1,176,2048]{2,1,0:T(8,128)(2,1)} %param.27, bf16[1,2048,176]{1,2,0:T(8,128)(2,1)} %param.26, bf16[64,1,3,2048]{3,2,1,0:T(4,128)(2,1)S(1)} %all_to_all.10, f32[64,1,3,176]{3,0,2,1:T(8,128)S(1)} %convolution_bitcast_fusion.2), kind=kOutput, calls=%fused_computation.3 | convolution fusion | flops 277420032 | bytes 3149824 | tf_op jit(solution)/shard_map/secf,efd->secd/dot_general | solution.py:59
  102.8 0.0 copy-start.8
  102.8 1.7 copy.73
  104.5 7.8 %all-to-all-start.1 = ((bf16[64,1,3,2048]{3,2,1,0:T(4,128)(2,1)}), bf16[64,1,3,2048]{3,2,1,0:T(4,128)(2,1)S(1)}, u32[]{:S(2)}, u32[]{:S(2)}) async-start(bf16[64,1,3,2048]{3,2,1,0:T(4,128)(2,1)} %copy.73), calls=%async_computation.1 | async-start | bytes 2097152 | tf_op jit(solution)/shard_map/all_to_all | solution.py:97
  112.2 0.0 reduce-scatter.2.cloned.1.call-start
  112.3 0.0 copy-done.8
  112.3 0.1 select_reduce_fusion
  112.4 26.8 %all-to-all-done.1 = bf16[64,1,3,2048]{3,2,1,0:T(4,128)(2,1)S(1)} async-done(((bf16[64,1,3,2048]{3,2,1,0:T(4,128)(2,1)}), bf16[64,1,3,2048]{3,2,1,0:T(4,128)(2,1)S(1)}, u32[]{:S(2)}, u32[]{:S(2)}) %all-to-all-start.1) | async-done | bytes 786464 | tf_op jit(solution)/shard_map/all_to_all | solution.py:97
  139.2 0.7 reshape.126
  139.9 1.1 convolution_convert_fusion.2
  140.9 0.0 reduce-scatter.2.cloned.1.call-update
  141.0 35.2 %reduce-scatter.2.cloned.1.call-done = bf16[20,256]{1,0:T(8,128)(2,1)} async-done(((bf16[20,2048]{1,0:T(8,128)(2,1)}), bf16[20,256]{1,0:T(8,128)(2,1)}) %reduce-scatter.2.cloned.1.call-update) | async-done | bytes 10256 | tf_op jit(solution)/shard_map/reduce_scatter | solution.py:106
  176.2 1.3 add_convert_fusion
  (14 shorter events, 0.2 us)
Async XLA Ops:
  6.5 4.4 %copy-start = (bf16[256,2048]{1,0:T(8,128)(2,1)S(1)}, bf16[256,2048]{1,0:T(8,128)(2,1)}, u32[]{:S(2)}) copy-start(bf16[256,2048]{1,0:T(8,128)(2,1)} %param.21) | copy-start | bytes 3145732
  6.5 52.2 %all-gather.4.cloned.1.call-start = ((), (), s32[]{:S(2)}) async-start(), calls=%async_computation.4 | async-start | bytes 1769472 | tf_op jit(solution)/shard_map/all_gather | solution.py:86
  6.5 2.1 %copy-start.4 = (bf16[20,256]{1,0:T(8,128)(2,1)S(1)}, bf16[20,256]{1,0:T(8,128)(2,1)}, u32[]{:S(2)}) copy-start(bf16[20,256]{1,0:T(8,128)(2,1)} %param.15) | copy-start | bytes 30724
  6.6 2.1 %copy-start.9 = (s32[4]{0:T(128)S(1)}, s32[4]{0:T(128)}, u32[]{:S(2)}) copy-start(s32[4]{0:T(128)} %param.19) | copy-start | bytes 52
  6.6 2.2 %copy-start.5 = (bf16[20,256]{1,0:T(8,128)(2,1)S(1)}, bf16[20,256]{1,0:T(8,128)(2,1)}, u32[]{:S(2)}) copy-start(bf16[20,256]{1,0:T(8,128)(2,1)} %param.14) | copy-start | bytes 30724
  6.6 2.2 %copy-start.1 = (bf16[4,384,256]{2,1,0:T(8,128)(2,1)S(1)}, bf16[4,384,256]{2,1,0:T(8,128)(2,1)}, u32[]{:S(2)}) copy-start(bf16[4,384,256]{2,1,0:T(8,128)(2,1)} %param.18) | copy-start | bytes 2359300
  8.8 0.8 copy-start.6
  10.3 1.7 copy-start.3
  11.0 49.3 %copy-start.2 = (bf16[20,2048]{1,0:T(8,128)(2,1)S(1)}, bf16[20,2048]{1,0:T(8,128)(2,1)}, u32[]{:S(2)}) copy-start(bf16[20,2048]{1,0:T(8,128)(2,1)} %param.20) | copy-start | bytes 245764
  11.9 48.5 %copy-start.7 = (f32[2048]{0:T(1024)S(1)}, f32[2048]{0:T(1024)}, u32[]{:S(2)}) copy-start(f32[2048]{0:T(1024)} %param.22) | copy-start | bytes 24580
  61.4 37.8 %copy-start.10 = (bf16[1,2048,176]{1,2,0:T(8,128)(2,1)S(1)}, bf16[1,2048,176]{1,2,0:T(8,128)(2,1)}, u32[]{:S(2)}) copy-start(bf16[1,2048,176]{1,2,0:T(8,128)(2,1)} %param.25) | copy-start | bytes 2162692
  102.8 9.5 %copy-start.8 = (f32[20,6]{0,1:T(8,128)S(1)}, f32[20,6]{0,1:T(8,128)}, u32[]{:S(2)}) copy-start(f32[20,6]{0,1:T(8,128)} %param.24) | copy-start | bytes 1444
  104.5 34.7 %all-to-all-start.1 = ((bf16[64,1,3,2048]{3,2,1,0:T(4,128)(2,1)}), bf16[64,1,3,2048]{3,2,1,0:T(4,128)(2,1)S(1)}, u32[]{:S(2)}, u32[]{:S(2)}) async-start(bf16[64,1,3,2048]{3,2,1,0:T(4,128)(2,1)} %copy.73), calls=%async_computation.1 | async-start | bytes 2097152 | tf_op jit(solution)/shard_map/all_to_all | solution.py:97
  112.2 63.9 %reduce-scatter.2.cloned.1.call-start = ((), (), s32[]{:S(2)}) async-start(), calls=%async_computation.3 | async-start | bytes 110592 | tf_op jit(solution)/shard_map/reduce_scatter | solution.py:106
Sparse Core Ops, SparseCore 0:
  12.0 46.6 all-gather.3
  141.1 35.0 reduce-scatter.1
